TPU v7x, 512 devices: a whole 4x8x8 slice. The times are simulated.
512 devices in a mesh: ctx: 64 (over z, y), section: 2 (over x_hi), dp: 4 (over x_lo, core).
Axes of the slice: x: 4 (x_hi: 2, x_lo: 2; x = x_hi * 2 + x_lo), y: 8, z: 8, core: 2. Of those that a mesh axis runs over, the one named last changes fastest.
Arguments:
- query_vectors: bfloat16 [4, 8192, 1792], P('dp', 'ctx', 'section'), may hold values from -16 to 16
- key_vectors: bfloat16 [4, 8192, 256], P('dp', 'ctx', 'section'), may hold values from -16 to 16
- value_vectors: bfloat16 [4, 8192, 256], P('dp', 'ctx', 'section'), may hold values from -6 to 6
- grad_output: bfloat16 [4, 8192, 1792], P('dp', 'ctx', 'section'), may hold values from -24 to 24
- output_dots: float32 [4, 14, 8192], P('dp', 'section', 'ctx'), may hold values from -12 to 12
- frame_ids: int32 [4, 8192], P('dp'), may hold values from 0 to 63, never falling along the last dimension, each value on 1 to 256 neighbouring positions
- visual_rows: int32 [4, 64, 32], P('dp', 'ctx'), may hold values from 0 to 127, as said below
- shuffle_source: int32 [4, 128, 64], P('dp', ('ctx', 'section')), may hold values from 0 to 63, each once within a row
- qkv_weight: bfloat16 [2304, 3584], P(None, ('section', 'dp')), may hold values from -0.125 to 0.125
- projector_weight: bfloat16 [3584, 2560], P(('section', 'dp')), may hold values from -0.09375 to 0.09375
Outputs:
- grad_keys: bfloat16 [4, 8192, 256], P('dp', 'ctx', 'section')
- grad_values: bfloat16 [4, 8192, 256], P('dp', 'ctx', 'section')
- patch_grads: bfloat16 [4, 8192, 640], P('dp', ('ctx', 'section'))
Inputs may be any that keep to these rules, and one draw needn't show every extreme that they name: `frame_ids`: frame numbers never fall along a sequence; a frame holds 1 to 256 tokens. `visual_rows`: each block of 128 tokens lists 32 distinct positions in increasing order. `shuffle_source`: each row is a permutation.
All inputs are finite; a program needn't handle non-finite values.
Results may differ from a plain program's by a relative error of at most 0.014.
Values may be sent and summed in bfloat16 or wider, within the bound.
No kernel may reach another device: no remote copies, remote signals or barrier semaphores. Data moves between devices by JAX's collectives and lax.ppermute only.
A program may use at most 128 MiB of HBM per device.

v0:
```python
import math
import jax
import jax.numpy as jnp
from jax import lax
from jax.sharding import PartitionSpec as P

HEAD_DIM = 128
GROUP = 7
MASKED = -1e30


def shards(
    query_vectors,
    key_vectors,
    value_vectors,
    grad_output,
    output_dots,
    frame_ids,
    visual_rows,
    shuffle_source,
    qkv_weight,
    projector_weight,
):
    ring_z = lax.axis_size("cz")
    ring_y = lax.axis_size("cy")
    position = lax.axis_index("cz") * ring_y + lax.axis_index("cy")
    local_rows = query_vectors.shape[1]
    scale_factor = 1.0 / math.sqrt(HEAD_DIM)
    query_heads = query_vectors[0].reshape(local_rows, GROUP, HEAD_DIM)
    grad_heads = grad_output[0].reshape(local_rows, GROUP, HEAD_DIM)
    corrections = output_dots[0]
    frame_line = frame_ids[0]
    seq_total = frame_line.shape[0]
    query_first = position * local_rows
    query_pos = query_first + jnp.arange(local_rows, dtype=jnp.int32)
    query_frames = lax.dynamic_slice_in_dim(frame_line, query_first, local_rows)
    own_pair = jnp.concatenate([key_vectors[0], value_vectors[0]], axis=1)
    all_pairs = lax.all_gather(
        lax.all_to_all(jnp.tile(own_pair, (ring_z, 1)), "cz", 0, 0, tiled=True),
        "cy",
        axis=0,
        tiled=True,
    )
    key_all = all_pairs[:, :HEAD_DIM]
    value_all = all_pairs[:, HEAD_DIM:]
    key_pos = (
        jnp.arange(seq_total, dtype=jnp.int32)
        .reshape(ring_z, ring_y, local_rows)
        .transpose(1, 0, 2)
        .reshape(seq_total)
    )
    key_frames = (
        frame_line.reshape(ring_z, ring_y, local_rows).transpose(1, 0, 2).reshape(seq_total)
    )
    allowed = (key_pos[None, :] <= query_pos[:, None]) | (
        key_frames[None, :] == query_frames[:, None]
    )
    scores = (
        jnp.einsum("qhd,kd->hqk", query_heads, key_all, preferred_element_type=jnp.float32)
        * scale_factor
    )
    masked_scores = jnp.where(allowed[None], scores, MASKED)
    running = masked_scores.max(axis=-1)
    summed = jnp.exp(masked_scores - running[:, :, None]).sum(axis=-1)
    log_total = running + jnp.log(summed)
    probability = jnp.exp(jnp.where(allowed[None], scores - log_total[:, :, None], MASKED))
    probs_low = probability.astype(jnp.bfloat16)
    grad_probs = jnp.einsum(
        "qhd,kd->hqk", grad_heads, value_all, preferred_element_type=jnp.float32
    )
    grad_scores = (probability * (grad_probs - corrections[:, :, None])).astype(jnp.bfloat16)
    grad_query = (
        jnp.einsum("hqk,kd->qhd", grad_scores, key_all, preferred_element_type=jnp.float32)
        * scale_factor
    )
    key_part = (
        jnp.einsum("hqk,qhd->kd", grad_scores, query_heads, preferred_element_type=jnp.float32)
        * scale_factor
    )
    value_part = jnp.einsum(
        "hqk,qhd->kd", probs_low, grad_heads, preferred_element_type=jnp.float32
    )
    stage_one = lax.psum_scatter(
        jnp.concatenate([key_part, value_part], axis=1).astype(jnp.bfloat16),
        "cy",
        scatter_dimension=0,
        tiled=True,
    )
    stage_two = lax.all_to_all(stage_one, "cz", 0, 0, tiled=True)
    summed_grads = (
        stage_two.astype(jnp.float32).reshape(ring_z, local_rows, stage_two.shape[1]).sum(0)
    )
    grad_keys_low = summed_grads[:, :HEAD_DIM].astype(jnp.bfloat16)
    grad_values_low = summed_grads[:, HEAD_DIM:].astype(jnp.bfloat16)
    grad_query_low = grad_query.astype(jnp.bfloat16).reshape(local_rows, GROUP * HEAD_DIM)
    visual_picks = visual_rows[0, 0]
    chosen = jnp.concatenate(
        [grad_query_low[visual_picks], grad_keys_low[visual_picks], grad_values_low[visual_picks]],
        axis=1,
    )
    everyone = lax.all_gather(chosen[None], ("section", "dp"), axis=0, tiled=True)
    groups = lax.axis_size("section")
    replicas = lax.axis_size("dp")
    half_rows = visual_picks.shape[0] // 2
    width_in = chosen.shape[1]
    arranged = (
        everyone.reshape(groups, replicas, 2, half_rows, width_in)
        .transpose(2, 1, 3, 0, 4)
        .reshape(2 * replicas * half_rows, groups * width_in)
    )
    visual_grad = jnp.dot(arranged, qkv_weight, preferred_element_type=jnp.float32).astype(
        jnp.bfloat16
    )
    pieces = lax.all_to_all(
        jnp.dot(visual_grad, projector_weight, preferred_element_type=jnp.float32).astype(
            jnp.bfloat16
        ),
        ("section", "dp"),
        0,
        0,
        tiled=True,
    )
    shuffled = pieces.astype(jnp.float32).reshape(groups * replicas, -1, pieces.shape[1]).sum(0)
    slot_rows = shuffled.reshape(half_rows * 4, projector_weight.shape[1] // 4)
    patches = slot_rows[shuffle_source[0, 0]].astype(jnp.bfloat16)
    return (grad_keys_low[None], grad_values_low[None], patches[None])


def solution(mesh):
    ctx_size = mesh.shape["ctx"]
    ring_y = 8 if ctx_size % 8 == 0 else 1
    split_mesh = jax.sharding.Mesh(
        mesh.devices.reshape(ctx_size // ring_y, ring_y, mesh.shape["section"], mesh.shape["dp"]),
        ("cz", "cy", "section", "dp"),
    )
    ctx = ("cz", "cy")
    placed = (
        P("dp", ctx, "section"),
        P("dp", ctx, "section"),
        P("dp", ctx, "section"),
        P("dp", ctx, "section"),
        P("dp", "section", ctx),
        P("dp", None),
        P("dp", ctx, None),
        P("dp", ("cz", "cy", "section"), None),
        P(None, ("section", "dp")),
        P(("section", "dp"), None),
    )
    return jax.shard_map(
        shards,
        mesh=split_mesh,
        in_specs=placed,
        out_specs=(
            P("dp", ctx, "section"),
            P("dp", ctx, "section"),
            P("dp", ("cz", "cy", "section"), None),
        ),
        check_vma=False,
    )
```

profile of v0, /device:TPU:1, one launch (start us, length us, event | category | flops | bytes accessed | tf_op | source)
XLA Modules:
  0.0 288.4 jit_solution(3191562445234428152)
XLA Ops:
  7.2 0.0 copy-start
  7.2 0.0 all-gather.3.cloned.1.call-start
  7.2 0.9 pad_maximum_fusion.2
  8.2 26.8 %all_to_all.27 = bf16[8,128,256]{2,1,0:T(8,128)(2,1)} all-to-all(bf16[8,128,256]{2,1,0:T(8,128)(2,1)S(1)} %tile.2), channel_id=1, replica_groups=mesh['cz'=8,'cy'=8,'section'=2,'dp'=4] {'cz'}, dimensions={0} | all-to-all | bytes 1048576 | tf_op jit(solution)/shard_map/all_to_all | solution.py:39
  35.0 0.0 all-gather.3.cloned.1.call-update
  35.0 0.0 reduce-scatter.2.cloned.1.call-start
  35.0 1.8 copy.46
  36.8 1.8 copy.44
  38.6 0.7 copy.74
  39.3 0.7 dynamic-slice_bitcast_fusion
  39.9 0.8 copy_bitcast_fusion.1
  40.7 2.8 compare_or_fusion
  43.5 46.8 %all-gather.3.cloned.1.call-done = bf16[8192,256]{1,0:T(8,128)(2,1)} async-done(((bf16[1024,256]{1,0:T(8,128)(2,1)}), bf16[8192,256]{1,0:T(8,128)(2,1)}) %all-gather.3.cloned.1.call-update) | async-done | bytes 4194320 | tf_op jit(solution)/shard_map/all_gather | solution.py:38
  90.2 13.1 %fusion.4 = (f32[7,128]{1,0:T(8,128)S(1)}, f32[8192,128,7]{1,0,2:T(8,128)}) fusion(pred[128,8192]{0,1:T(8,128)(4,1)S(1)} %compare_or_fusion, bf16[128,7,128]{0,2,1:T(8,128)(2,1)} %bitcast.113, bf16[8192,256]{1,0:T(8,128)(2,1)} %all-gather.3.cloned.1.call-done), kind=kOutput, calls=%fused_computation.12 | convolution fusion | flops 1901067392 | bytes 32738816 | tf_op jit(solution)/shard_map/qhd,kd->hqk/dot_general | solution.py:59
  103.4 12.7 %exponential_reduce_fusion = f32[7,128]{1,0:T(8,128)S(1)} fusion(f32[8192,128,7]{1,0,2:T(8,128)} %get-tuple-element.6, f32[7,128]{1,0:T(8,128)S(1)} %get-tuple-element.5, pred[128,8192]{0,1:T(8,128)(4,1)S(1)} %compare_or_fusion), kind=kLoop, calls=%fused_computation.11 | loop fusion | flops 29359232 | bytes 30415872 | tf_op jit(solution)/shard_map/reduce_sum | solution.py:64
  116.1 0.0 copy-done.4
  116.1 0.0 copy-start.1
  116.1 13.4 %fusion.13 = bf16[8192,128]{0,1:T(8,128)(2,1)S(1)} fusion(bf16[128,7,128]{0,2,1:T(8,128)(2,1)S(1)} %bitcast.111, f32[8192,128,7]{1,0,2:T(8,128)} %get-tuple-element.6, f32[7,128]{1,0:T(8,128)S(1)} %log_add_fusion, pred[128,8192]{0,1:T(8,128)(4,1)S(1)} %compare_or_fusion), kind=kOutput, calls=%fused_computation.19 | convolution fusion | flops 1909456896 | bytes 32738816 | tf_op jit(solution)/shard_map/hqk,qhd->kd/dot_general | solution.py:80
  129.5 0.0 copy-done.1
  129.5 19.4 %fusion.1 = bf16[7,128,8192]{1,2,0:T(8,128)(2,1)} fusion(f32[8192,128,7]{1,0,2:T(8,128)} %get-tuple-element.6, bf16[128,7,128]{0,2,1:T(8,128)(2,1)S(1)} %bitcast.112, f32[7,128]{1,0:T(8,128)S(1)} %bitcast.119, f32[7,128]{1,0:T(8,128)S(1)} %log_add_fusion, pred[128,8192]{0,1:T(8,128)(4,1)S(1)} %compare_or_fusion, bf16[8192,256]{1,0:T(8,128)(2,1)S(1)} %copy-done.1), kind=kOutput, calls=%fused_computation.6 | convolution fusion | flops 1923088384 | bytes 47423488 | tf_op jit(solution)/shard_map/qhd,kd->hqk/dot_general | solution.py:68
  148.9 9.9 %fusion.16 = bf16[8192,128]{0,1:T(8,128)(2,1)S(1)} fusion(bf16[7,128,8192]{1,2,0:T(8,128)(2,1)} %fusion.1, bf16[128,7,128]{0,2,1:T(8,128)(2,1)S(1)} %bitcast.114), kind=kOutput, calls=%fused_computation.20 | convolution fusion | flops 1881145344 | bytes 17006592 | tf_op jit(solution)/shard_map/hqk,qhd->kd/dot_general | solution.py:77
  158.8 0.0 copy-start.6
  158.8 2.4 pad_maximum_fusion
  161.2 0.0 reduce-scatter.2.cloned.1.call-update
  161.3 56.8 %reduce-scatter.2.cloned.1.call-done = bf16[1024,256]{0,1:T(8,128)(2,1)} async-done(((bf16[8192,256]{0,1:T(8,128)(2,1)}), bf16[1024,256]{0,1:T(8,128)(2,1)}) %reduce-scatter.2.cloned.1.call-update) | async-done | bytes 524304 | tf_op jit(solution)/shard_map/reduce_scatter | solution.py:83
  218.1 1.9 copy_bitcast_fusion
  220.0 7.1 %all-to-all-start.1 = ((bf16[8,128,256]{1,2,0:T(8,128)(2,1)}), bf16[8,128,256]{1,2,0:T(8,128)(2,1)S(1)}, u32[]{:S(2)}, u32[]{:S(2)}) async-start(bf16[8,128,256]{1,2,0:T(8,128)(2,1)} %copy_bitcast_fusion), calls=%async_computation.2 | async-start | bytes 1048576 | tf_op jit(solution)/shard_map/all_to_all | solution.py:89
  227.1 8.2 %fusion.20 = bf16[128,7,128]{2,0,1:T(8,128)(2,1)S(1)} fusion(bf16[7,128,8192]{1,2,0:T(8,128)(2,1)} %fusion.1, bf16[8192,256]{1,0:T(8,128)(2,1)} %all-gather.3.cloned.1.call-done), kind=kOutput, calls=%fused_computation.30 | convolution fusion | flops 1879277568 | bytes 17006592 | tf_op jit(solution)/shard_map/hqk,kd->qhd/dot_general | solution.py:73
  235.3 0.0 copy-start.7
  235.3 0.2 copy.56
  235.5 0.6 gather_fusion
  236.1 8.9 %all-to-all-done.1 = bf16[8,128,256]{1,2,0:T(8,128)(2,1)S(1)} async-done(((bf16[8,128,256]{1,2,0:T(8,128)(2,1)}), bf16[8,128,256]{1,2,0:T(8,128)(2,1)S(1)}, u32[]{:S(2)}, u32[]{:S(2)}) %all-to-all-start.1) | async-done | bytes 524320 | tf_op jit(solution)/shard_map/all_to_all | solution.py:89
  245.1 0.1 reduce
  245.2 0.1 copy.67
  245.3 0.0 copy-start.2
  245.3 0.1 copy.68
  245.4 0.0 copy-start.3
  245.4 0.6 gather_fusion.2
  246.0 0.6 gather_fusion.1
  246.6 13.8 %all-gather = bf16[256,1152]{1,0:T(8,128)(2,1)S(1)} all-gather(bf16[32,1152]{1,0:T(8,128)(2,1)S(1)} %pad_maximum_fusion.1), channel_id=2, replica_groups=mesh['cz'=8,'cy'=8,'section'=2,'dp'=4] {'section','dp'}, dimensions={0}, use_global_device_ids=true | all-gather | bytes 663552 | tf_op jit(solution)/shard_map/all_gather | solution.py:101
  260.4 0.6 copy.57
  261.1 0.1 copy.70
  261.1 4.2 %convolution_convert_fusion = bf16[128,2560]{1,0:T(8,128)(2,1)} fusion(bf16[448,2560]{1,0:T(8,128)(2,1)S(1)} %copy-done, bf16[128,2304]{1,0:T(8,128)(2,1)S(1)} %bitcast.106, bf16[2304,448]{0,1:T(8,128)(2,1)} %param.18), kind=kOutput, calls=%fused_computation.23 | convolution fusion | flops 558227456 | bytes 5603328 | tf_op jit(solution)/shard_map/dot_general | solution.py:115
  265.4 3.8 %all-to-all-start.2 = ((bf16[8,16,2560]{2,1,0:T(8,128)(2,1)}), bf16[8,16,2560]{2,1,0:T(8,128)(2,1)S(1)}, u32[]{:S(2)}, u32[]{:S(2)}) async-start(bf16[8,16,2560]{2,1,0:T(8,128)(2,1)} %bitcast.103), calls=%async_computation.3 | async-start | bytes 1310720 | tf_op jit(solution)/shard_map/all_to_all | solution.py:114
  269.2 10.9 %all-to-all-done.2 = bf16[8,16,2560]{2,1,0:T(8,128)(2,1)S(1)} async-done(((bf16[8,16,2560]{2,1,0:T(8,128)(2,1)}), bf16[8,16,2560]{2,1,0:T(8,128)(2,1)S(1)}, u32[]{:S(2)}, u32[]{:S(2)}) %all-to-all-start.2) | async-done | bytes 655392 | tf_op jit(solution)/shard_map/all_to_all | solution.py:114
  280.1 0.1 convert_reduce_fusion
  280.2 0.1 reshape.222
  280.2 1.3 gather_fusion.3
  (17 shorter events, 0.1 us)
Async XLA Ops:
  7.2 254.0 %copy-start = (bf16[448,2560]{1,0:T(8,128)(2,1)S(1)}, bf16[448,2560]{1,0:T(8,128)(2,1)}, u32[]{:S(2)}) copy-start(bf16[448,2560]{1,0:T(8,128)(2,1)} %param.19) | copy-start | bytes 6881284
  7.2 83.1 %all-gather.3.cloned.1.call-start = ((), (), s32[]{:S(2)}) async-start(), calls=%async_computation.4 | async-start | bytes 4718592 | tf_op jit(solution)/shard_map/all_gather | solution.py:38
  35.0 183.1 %reduce-scatter.2.cloned.1.call-start = ((), (), s32[]{:S(2)}) async-start(), calls=%async_computation.5 | async-start | bytes 4718592 | tf_op jit(solution)/shard_map/reduce_scatter | solution.py:83
  103.4 12.7 %copy-start.4 = (bf16[1,128,896]{1,2,0:T(8,128)(2,1)S(1)}, bf16[1,128,896]{1,2,0:T(8,128)(2,1)}, u32[]{:S(2)}) copy-start(bf16[1,128,896]{1,2,0:T(8,128)(2,1)} %copy.46) | copy-start | bytes 688132
  116.1 13.4 %copy-start.1 = (bf16[8192,256]{1,0:T(8,128)(2,1)S(1)}, bf16[8192,256]{1,0:T(8,128)(2,1)}, u32[]{:S(2)}) copy-start(bf16[8192,256]{1,0:T(8,128)(2,1)} %all-gather.3.cloned.1.call-done) | copy-start | bytes 12582916
  129.5 19.4 %copy-start.5 = (bf16[1,128,896]{1,2,0:T(8,128)(2,1)S(1)}, bf16[1,128,896]{1,2,0:T(8,128)(2,1)}, u32[]{:S(2)}) copy-start(bf16[1,128,896]{1,2,0:T(8,128)(2,1)} %copy.44) | copy-start | bytes 688132
  158.8 2.4 copy-start.6
  220.0 25.1 %all-to-all-start.1 = ((bf16[8,128,256]{1,2,0:T(8,128)(2,1)}), bf16[8,128,256]{1,2,0:T(8,128)(2,1)S(1)}, u32[]{:S(2)}, u32[]{:S(2)}) async-start(bf16[8,128,256]{1,2,0:T(8,128)(2,1)} %copy_bitcast_fusion), calls=%async_computation.2 | async-start | bytes 1048576 | tf_op jit(solution)/shard_map/all_to_all | solution.py:89
  235.3 33.9 %copy-start.7 = (s32[1,1,64]{2,1,0:T(1,128)S(1)}, s32[1,1,64]{2,1,0:T(1,128)}, u32[]{:S(2)}) copy-start(s32[1,1,64]{2,1,0:T(1,128)} %param.17) | copy-start | bytes 772
  245.3 36.3 %copy-start.2 = (bf16[128,128]{1,0:T(8,128)(2,1)}, bf16[128,128]{1,0:T(8,128)(2,1)S(1)}, u32[]{:S(2)}) copy-start(bf16[128,128]{1,0:T(8,128)(2,1)S(1)} %copy.67) | copy-start | bytes 98308
  245.4 36.2 %copy-start.3 = (bf16[128,128]{1,0:T(8,128)(2,1)}, bf16[128,128]{1,0:T(8,128)(2,1)S(1)}, u32[]{:S(2)}) copy-start(bf16[128,128]{1,0:T(8,128)(2,1)S(1)} %copy.68) | copy-start | bytes 98308
  265.4 14.7 %all-to-all-start.2 = ((bf16[8,16,2560]{2,1,0:T(8,128)(2,1)}), bf16[8,16,2560]{2,1,0:T(8,128)(2,1)S(1)}, u32[]{:S(2)}, u32[]{:S(2)}) async-start(bf16[8,16,2560]{2,1,0:T(8,128)(2,1)} %bitcast.103), calls=%async_computation.3 | async-start | bytes 1310720 | tf_op jit(solution)/shard_map/all_to_all | solution.py:114
Sparse Core Ops, SparseCore 0:
  35.1 55.0 all-gather.2
  161.4 56.6 reduce-scatter.1
where the time goes:
time: 289 us; the launch traced here: 288 us
  waiting for transfers between devices  123 us (43%)
  matrix products  68.2 us (24%)
  blocking collectives  40.6 us (14%)
  other arithmetic  19.8 us (7%)
  between operations  14.3 us (5%)
  local copies, waits for them, and re-layouts  11.2 us (4%)
  starting transfers between devices  11 us (4%)
    reduce_scatter x1, waiting for transfers between devices, shards(): lax.psum_scatter(jnp.concatenate([key_part, value_part], axis=1).astype(j...  56.8 us
    all_gather x1, waiting for transfers between devices, shards(): lax.all_gather(lax.all_to_all(jnp.tile(own_pair, (ring_z, 1)), 'cz', 0, 0...  46.8 us
    all_to_all x1, blocking collectives, shards(): lax.all_to_all(jnp.tile(own_pair, (ring_z, 1)), 'cz', 0, 0, tiled=True)  26.8 us
    dot_general x1, matrix products, shards(): jnp.einsum('qhd,kd->hqk', grad_heads, value_all, preferred_element_type=j...  19.4 us
    all_gather x1, blocking collectives, shards(): lax.all_gather(chosen[None], ('section', 'dp'), axis=0, tiled=True)  13.8 us
    dot_general x1, matrix products, shards(): jnp.einsum('hqk,qhd->kd', probs_low, grad_heads, preferred_element_type=j...  13.4 us
    dot_general x1, matrix products, shards(): jnp.einsum('qhd,kd->hqk', query_heads, key_all, preferred_element_type=jn...  13.1 us
    reduce_sum x1, other arithmetic, shards(): summed = jnp.exp(masked_scores - running[:, :, None]).sum(axis=-1)  12.7 us
  transfers between devices with their start and end apart: 4, of which 4 were waited for; matrix products, arithmetic and copies ran while one was open for 6% of the time, Pallas kernels for 0%

commit v1 on v0

--- a/solution.py
+++ b/solution.py
@@ -35,12 +35,11 @@
     query_pos = query_first + jnp.arange(local_rows, dtype=jnp.int32)
     query_frames = lax.dynamic_slice_in_dim(frame_line, query_first, local_rows)
     own_pair = jnp.concatenate([key_vectors[0], value_vectors[0]], axis=1)
-    all_pairs = lax.all_gather(
-        lax.all_to_all(jnp.tile(own_pair, (ring_z, 1)), "cz", 0, 0, tiled=True),
-        "cy",
-        axis=0,
-        tiled=True,
-    )
+    block = lax.all_to_all(jnp.tile(own_pair, (ring_z, 1)), "cz", 0, 0, tiled=True)
+    devices = lax.axis_size("cy")
+    blocks = jnp.stack([block for _ in range(devices)])
+    blocks = lax.all_to_all(blocks, "cy", split_axis=0, concat_axis=0)
+    all_pairs = jnp.concatenate(blocks, axis=0)
     key_all = all_pairs[:, :HEAD_DIM]
     value_all = all_pairs[:, HEAD_DIM:]
     key_pos = (

time: 289 us -> 333 us (1.15)
  waiting for transfers between devices: 123 us -> 162 us
  starting transfers between devices: 11 us -> 17.8 us
    all_to_all x0 -> x1, waiting for transfers between devices: none -> 92.2 us  [shards(): blocks = lax.all_to_all(blocks, 'cy', split_axis=0, concat_axis=0)]
    all_gather x1 -> x0, waiting for transfers between devices: 46.8 us -> none  [shards(): lax.all_gather(lax.all_to_all(jnp.tile(own_pair, (ring_z, 1)), 'cz', 0, 0...]
    reduce_scatter x1, waiting for transfers between devices: 56.8 us -> 49.8 us  [shards(): lax.psum_scatter(jnp.concatenate([key_part, value_part], axis=1).astype(j...]
    all_to_all x0 -> x1, starting transfers between devices: none -> 6.82 us  [shards(): blocks = lax.all_to_all(blocks, 'cy', split_axis=0, concat_axis=0)]
  transfers between devices with their start and end apart: 4 -> 4, of which waited for: 4 -> 4; matrix products, arithmetic and copies ran while one was open for 6% -> 4% of each run, Pallas kernels for 0% -> 0%
where the time goes in v1:
time: 333 us; the launch traced here: 332 us
  waiting for transfers between devices  162 us (49%)
  matrix products  68.4 us (21%)
  blocking collectives  40.5 us (12%)
  other arithmetic  19 us (6%)
  starting transfers between devices  17.8 us (5%)
  between operations  14.3 us (4%)
  local copies, waits for them, and re-layouts  10.2 us (3%)
    all_to_all x1, waiting for transfers between devices, shards(): blocks = lax.all_to_all(blocks, 'cy', split_axis=0, concat_axis=0)  92.2 us
    reduce_scatter x1, waiting for transfers between devices, shards(): lax.psum_scatter(jnp.concatenate([key_part, value_part], axis=1).astype(j...  49.8 us
    all_to_all x1, blocking collectives, shards(): lax.all_to_all(jnp.tile(own_pair, (ring_z, 1)), 'cz', 0, 0, tiled=True)  26.7 us
    dot_general x1, matrix products, shards(): jnp.einsum('qhd,kd->hqk', grad_heads, value_all, preferred_element_type=j...  19.8 us
    all_gather x1, blocking collectives, shards(): lax.all_gather(chosen[None], ('section', 'dp'), axis=0, tiled=True)  13.8 us
    dot_general x1, matrix products, shards(): jnp.einsum('hqk,qhd->kd', probs_low, grad_heads, preferred_element_type=j...  13.2 us
    dot_general x1, matrix products, shards(): jnp.einsum('qhd,kd->hqk', query_heads, key_all, preferred_element_type=jn...  13.1 us
    reduce_sum x1, other arithmetic, shards(): summed = jnp.exp(masked_scores - running[:, :, None]).sum(axis=-1)  12.7 us
  transfers between devices with their start and end apart: 4, of which 4 were waited for; matrix products, arithmetic and copies ran while one was open for 4% of the time, Pallas kernels for 0%

profile of v1, /device:TPU:1, one launch (start us, length us, event | category | flops | bytes accessed | tf_op | source)
XLA Modules:
  0.0 332.1 jit_solution(7447790130765332575)
XLA Ops:
  7.2 0.0 copy-start
  7.2 0.9 pad_maximum_fusion.2
  8.2 26.7 %all_to_all.29 = bf16[8,128,256]{2,1,0:T(8,128)(2,1)S(1)} all-to-all(bf16[8,128,256]{2,1,0:T(8,128)(2,1)S(1)} %tile.2), channel_id=1, replica_groups=mesh['cz'=8,'cy'=8,'section'=2,'dp'=4] {'cz'}, dimensions={0} | all-to-all | bytes 1048576 | tf_op jit(solution)/shard_map/all_to_all | solution.py:38
  34.9 2.2 stack.5
  37.1 6.8 %all-to-all-start.1 = ((bf16[8,1024,256]{2,1,0:T(8,128)(2,1)}), bf16[8,1024,256]{2,1,0:T(8,128)(2,1)}, u32[]{:S(2)}, u32[]{:S(2)}) async-start(bf16[8,1024,256]{2,1,0:T(8,128)(2,1)} %stack.5), calls=%async_computation.1 | async-start | bytes 8388608 | tf_op jit(solution)/shard_map/all_to_all | solution.py:41
  43.9 0.0 reduce-scatter.2.cloned.1.call-start
  43.9 0.0 copy-done.3
  43.9 0.8 copy.46
  44.8 0.9 copy.44
  45.6 0.0 copy-done.8
  45.6 0.0 copy-done.7
  45.7 2.8 compare_or_fusion
  48.5 92.2 %all-to-all-done.1 = bf16[8,1024,256]{2,1,0:T(8,128)(2,1)} async-done(((bf16[8,1024,256]{2,1,0:T(8,128)(2,1)}), bf16[8,1024,256]{2,1,0:T(8,128)(2,1)}, u32[]{:S(2)}, u32[]{:S(2)}) %all-to-all-start.1) | async-done | bytes 4194336 | tf_op jit(solution)/shard_map/all_to_all | solution.py:41
  140.7 13.1 %fusion.4 = (f32[7,128]{1,0:T(8,128)S(1)}, f32[8192,128,7]{1,0,2:T(8,128)}) fusion(pred[128,8192]{0,1:T(8,128)(4,1)S(1)} %compare_or_fusion, bf16[128,7,128]{0,2,1:T(8,128)(2,1)} %bitcast.114, bf16[8192,256]{1,0:T(8,128)(2,1)} %bitcast.8), kind=kOutput, calls=%fused_computation.12 | convolution fusion | flops 1901067392 | bytes 32738816 | tf_op jit(solution)/shard_map/qhd,kd->hqk/dot_general | solution.py:58
  153.9 12.7 %exponential_reduce_fusion = f32[7,128]{1,0:T(8,128)S(1)} fusion(f32[8192,128,7]{1,0,2:T(8,128)} %get-tuple-element.6, f32[7,128]{1,0:T(8,128)S(1)} %get-tuple-element.5, pred[128,8192]{0,1:T(8,128)(4,1)S(1)} %compare_or_fusion), kind=kLoop, calls=%fused_computation.11 | loop fusion | flops 29359232 | bytes 30415872 | tf_op jit(solution)/shard_map/reduce_sum | solution.py:63
  166.6 0.0 copy-done.5
  166.6 13.2 %fusion.13 = bf16[8192,128]{0,1:T(8,128)(2,1)S(1)} fusion(bf16[128,7,128]{0,2,1:T(8,128)(2,1)S(1)} %bitcast.112, f32[8192,128,7]{1,0,2:T(8,128)} %get-tuple-element.6, f32[7,128]{1,0:T(8,128)S(1)} %log_add_fusion, pred[128,8192]{0,1:T(8,128)(4,1)S(1)} %compare_or_fusion), kind=kOutput, calls=%fused_computation.19 | convolution fusion | flops 1909456896 | bytes 32738816 | tf_op jit(solution)/shard_map/hqk,qhd->kd/dot_general | solution.py:79
  179.8 0.0 copy-start.6
  179.8 19.8 %fusion.1 = bf16[7,128,8192]{1,2,0:T(8,128)(2,1)} fusion(f32[8192,128,7]{1,0,2:T(8,128)} %get-tuple-element.6, bf16[128,7,128]{0,2,1:T(8,128)(2,1)S(1)} %bitcast.113, f32[7,128]{1,0:T(8,128)S(1)} %bitcast.120, f32[7,128]{1,0:T(8,128)S(1)} %log_add_fusion, pred[128,8192]{0,1:T(8,128)(4,1)S(1)} %compare_or_fusion, bf16[8192,256]{1,0:T(8,128)(2,1)} %bitcast.8), kind=kOutput, calls=%fused_computation.6 | convolution fusion | flops 1923088384 | bytes 47422464 | tf_op jit(solution)/shard_map/qhd,kd->hqk/dot_general | solution.py:67
  199.6 9.9 %fusion.16 = bf16[8192,128]{0,1:T(8,128)(2,1)S(1)} fusion(bf16[7,128,8192]{1,2,0:T(8,128)(2,1)} %fusion.1, bf16[128,7,128]{0,2,1:T(8,128)(2,1)S(1)} %bitcast.115), kind=kOutput, calls=%fused_computation.20 | convolution fusion | flops 1881145344 | bytes 17006592 | tf_op jit(solution)/shard_map/hqk,qhd->kd/dot_general | solution.py:76
  209.5 0.0 copy-start.9
  209.5 2.4 pad_maximum_fusion
  211.9 0.0 reduce-scatter.2.cloned.1.call-update
  211.9 0.0 copy-done.9
  212.0 49.8 %reduce-scatter.2.cloned.1.call-done = bf16[1024,256]{0,1:T(8,128)(2,1)} async-done(((bf16[8192,256]{0,1:T(8,128)(2,1)}), bf16[1024,256]{0,1:T(8,128)(2,1)}) %reduce-scatter.2.cloned.1.call-update) | async-done | bytes 524304 | tf_op jit(solution)/shard_map/reduce_scatter | solution.py:82
  261.8 1.9 copy_bitcast_fusion
  263.7 7.1 %all-to-all-start.2 = ((bf16[8,128,256]{1,2,0:T(8,128)(2,1)}), bf16[8,128,256]{1,2,0:T(8,128)(2,1)S(1)}, u32[]{:S(2)}, u32[]{:S(2)}) async-start(bf16[8,128,256]{1,2,0:T(8,128)(2,1)} %copy_bitcast_fusion), calls=%async_computation.3 | async-start | bytes 1048576 | tf_op jit(solution)/shard_map/all_to_all | solution.py:88
  270.8 8.2 %fusion.20 = bf16[128,7,128]{2,0,1:T(8,128)(2,1)S(1)} fusion(bf16[7,128,8192]{1,2,0:T(8,128)(2,1)} %fusion.1, bf16[8192,256]{1,0:T(8,128)(2,1)} %bitcast.8), kind=kOutput, calls=%fused_computation.30 | convolution fusion | flops 1879277568 | bytes 17006592 | tf_op jit(solution)/shard_map/hqk,kd->qhd/dot_general | solution.py:72
  279.0 0.0 copy-start.10
  279.0 0.2 copy.56
  279.2 0.6 gather_fusion
  279.8 8.9 %all-to-all-done.2 = bf16[8,128,256]{1,2,0:T(8,128)(2,1)S(1)} async-done(((bf16[8,128,256]{1,2,0:T(8,128)(2,1)}), bf16[8,128,256]{1,2,0:T(8,128)(2,1)S(1)}, u32[]{:S(2)}, u32[]{:S(2)}) %all-to-all-start.2) | async-done | bytes 524320 | tf_op jit(solution)/shard_map/all_to_all | solution.py:88
  288.8 0.1 reduce
  288.9 0.1 copy.67
  289.0 0.0 copy-start.1
  289.0 0.1 copy.68
  289.1 0.0 copy-start.2
  289.1 0.6 gather_fusion.2
  289.7 0.6 gather_fusion.1
  290.3 13.8 %all-gather = bf16[256,1152]{1,0:T(8,128)(2,1)S(1)} all-gather(bf16[32,1152]{1,0:T(8,128)(2,1)S(1)} %pad_maximum_fusion.1), channel_id=2, replica_groups=mesh['cz'=8,'cy'=8,'section'=2,'dp'=4] {'section','dp'}, dimensions={0}, use_global_device_ids=true | all-gather | bytes 663552 | tf_op jit(solution)/shard_map/all_gather | solution.py:100
  304.1 0.6 copy.57
  304.7 0.1 copy.70
  304.8 4.2 %convolution_convert_fusion = bf16[128,2560]{1,0:T(8,128)(2,1)} fusion(bf16[448,2560]{1,0:T(8,128)(2,1)S(1)} %copy-done, bf16[128,2304]{1,0:T(8,128)(2,1)S(1)} %bitcast.107, bf16[2304,448]{0,1:T(8,128)(2,1)} %param.18), kind=kOutput, calls=%fused_computation.23 | convolution fusion | flops 558227456 | bytes 5603328 | tf_op jit(solution)/shard_map/dot_general | solution.py:114
  309.0 3.8 %all-to-all-start.3 = ((bf16[8,16,2560]{2,1,0:T(8,128)(2,1)}), bf16[8,16,2560]{2,1,0:T(8,128)(2,1)S(1)}, u32[]{:S(2)}, u32[]{:S(2)}) async-start(bf16[8,16,2560]{2,1,0:T(8,128)(2,1)} %bitcast.104), calls=%async_computation.4 | async-start | bytes 1310720 | tf_op jit(solution)/shard_map/all_to_all | solution.py:113
  312.9 10.9 %all-to-all-done.3 = bf16[8,16,2560]{2,1,0:T(8,128)(2,1)S(1)} async-done(((bf16[8,16,2560]{2,1,0:T(8,128)(2,1)}), bf16[8,16,2560]{2,1,0:T(8,128)(2,1)S(1)}, u32[]{:S(2)}, u32[]{:S(2)}) %all-to-all-start.3) | async-done | bytes 655392 | tf_op jit(solution)/shard_map/all_to_all | solution.py:113
  323.7 0.1 convert_reduce_fusion
  323.8 0.1 reshape.229
  323.9 1.3 gather_fusion.3
  (23 shorter events, 0.1 us)
Async XLA Ops:
  7.2 297.6 %copy-start = (bf16[448,2560]{1,0:T(8,128)(2,1)S(1)}, bf16[448,2560]{1,0:T(8,128)(2,1)}, u32[]{:S(2)}) copy-start(bf16[448,2560]{1,0:T(8,128)(2,1)} %param.19) | copy-start | bytes 6881284
  7.2 36.7 %copy-start.3 = (bf16[1,128,896]{2,1,0:T(8,128)(2,1)S(1)}, bf16[1,128,896]{2,1,0:T(8,128)(2,1)}, u32[]{:S(2)}) copy-start(bf16[1,128,896]{2,1,0:T(8,128)(2,1)} %param.13) | copy-start | bytes 688132
  7.2 37.6 %copy-start.4 = (bf16[1,128,896]{2,1,0:T(8,128)(2,1)S(1)}, bf16[1,128,896]{2,1,0:T(8,128)(2,1)}, u32[]{:S(2)}) copy-start(bf16[1,128,896]{2,1,0:T(8,128)(2,1)} %param.10) | copy-start | bytes 688132
  7.2 38.4 %copy-start.8 = (f32[1,7,128]{2,0,1:T(1,128)S(1)}, f32[1,7,128]{2,0,1:T(1,128)}, u32[]{:S(2)}) copy-start(f32[1,7,128]{2,0,1:T(1,128)} %param.14) | copy-start | bytes 10756
  7.2 38.4 %copy-start.7 = (s32[1,8192]{1,0:T(1,128)S(1)}, s32[1,8192]{1,0:T(1,128)}, u32[]{:S(2)}) copy-start(s32[1,8192]{1,0:T(1,128)} %param.15) | copy-start | bytes 98308
  37.1 103.7 %all-to-all-start.1 = ((bf16[8,1024,256]{2,1,0:T(8,128)(2,1)}), bf16[8,1024,256]{2,1,0:T(8,128)(2,1)}, u32[]{:S(2)}, u32[]{:S(2)}) async-start(bf16[8,1024,256]{2,1,0:T(8,128)(2,1)} %stack.5), calls=%async_computation.1 | async-start | bytes 8388608 | tf_op jit(solution)/shard_map/all_to_all | solution.py:41
  43.9 217.9 %reduce-scatter.2.cloned.1.call-start = ((), (), s32[]{:S(2)}) async-start(), calls=%async_computation.5 | async-start | bytes 4718592 | tf_op jit(solution)/shard_map/reduce_scatter | solution.py:82
  153.9 12.7 %copy-start.5 = (bf16[1,128,896]{1,2,0:T(8,128)(2,1)S(1)}, bf16[1,128,896]{1,2,0:T(8,128)(2,1)}, u32[]{:S(2)}) copy-start(bf16[1,128,896]{1,2,0:T(8,128)(2,1)} %copy.46) | copy-start | bytes 688132
  179.8 19.8 %copy-start.6 = (bf16[1,128,896]{1,2,0:T(8,128)(2,1)S(1)}, bf16[1,128,896]{1,2,0:T(8,128)(2,1)}, u32[]{:S(2)}) copy-start(bf16[1,128,896]{1,2,0:T(8,128)(2,1)} %copy.44) | copy-start | bytes 688132
  209.5 2.4 copy-start.9
  263.7 25.1 %all-to-all-start.2 = ((bf16[8,128,256]{1,2,0:T(8,128)(2,1)}), bf16[8,128,256]{1,2,0:T(8,128)(2,1)S(1)}, u32[]{:S(2)}, u32[]{:S(2)}) async-start(bf16[8,128,256]{1,2,0:T(8,128)(2,1)} %copy_bitcast_fusion), calls=%async_computation.3 | async-start | bytes 1048576 | tf_op jit(solution)/shard_map/all_to_all | solution.py:88
  279.0 33.8 %copy-start.10 = (s32[1,1,64]{2,1,0:T(1,128)S(1)}, s32[1,1,64]{2,1,0:T(1,128)}, u32[]{:S(2)}) copy-start(s32[1,1,64]{2,1,0:T(1,128)} %param.17) | copy-start | bytes 772
  289.0 36.3 %copy-start.1 = (bf16[128,128]{1,0:T(8,128)(2,1)}, bf16[128,128]{1,0:T(8,128)(2,1)S(1)}, u32[]{:S(2)}) copy-start(bf16[128,128]{1,0:T(8,128)(2,1)S(1)} %copy.67) | copy-start | bytes 98308
  289.1 36.1 %copy-start.2 = (bf16[128,128]{1,0:T(8,128)(2,1)}, bf16[128,128]{1,0:T(8,128)(2,1)S(1)}, u32[]{:S(2)}) copy-start(bf16[128,128]{1,0:T(8,128)(2,1)S(1)} %copy.68) | copy-start | bytes 98308
  309.0 14.7 %all-to-all-start.3 = ((bf16[8,16,2560]{2,1,0:T(8,128)(2,1)}), bf16[8,16,2560]{2,1,0:T(8,128)(2,1)S(1)}, u32[]{:S(2)}, u32[]{:S(2)}) async-start(bf16[8,16,2560]{2,1,0:T(8,128)(2,1)} %bitcast.104), calls=%async_computation.4 | async-start | bytes 1310720 | tf_op jit(solution)/shard_map/all_to_all | solution.py:113
Sparse Core Ops, SparseCore 0:
  212.1 49.6 reduce-scatter.1
